TPU v7x, 512 devices: a whole 4x4x16 slice. The times are simulated.
512 devices in a mesh: dp: 32 (over z, core), expert: 16 (over x, y).
Axes of the slice: x: 4, y: 4, z: 16, core: 2. Of those that a mesh axis runs over, the one named last changes fastest.
Arguments:
- grad_out: bfloat16 [65536, 2048], P(('dp', 'expert')), may hold values from -6 to 6
- gate: float32 [65536, 1], P(('dp', 'expert')), may hold values from 0.25 to 1
- expert_ids: int32 [65536, 1], P(('dp', 'expert')), may hold values from 0 to 15; in each aligned block of 128 rows (0 to 127, 128 to 255, ...) at most 10 rows name the same one
- w_in: bfloat16 [16, 5120, 2048], P('expert', 'dp'), may hold values from -0.125 to 0.125
- w_out: bfloat16 [16, 5120, 2048], P('expert', 'dp'), may hold values from -0.078125 to 0.078125
- pre_act: bfloat16 [32, 16, 160, 5120], P('dp', 'expert'), may hold values from -6 to 6
Outputs:
- grad_in: bfloat16 [65536, 2048], P(('dp', 'expert'))
Inputs may be any that keep to these rules, and one draw needn't show every extreme that they name: `expert_ids`: among the 128 tokens of one device no expert is named more than 10 times, and in every draw some device names some expert exactly 10 times.
All inputs are finite; a program needn't handle non-finite values.
Results may differ from a plain program's by a relative error of at most 0.0057.
Values may be sent and summed in bfloat16 or wider, within the bound.
No kernel may reach another device: no remote copies, remote signals or barrier semaphores. Data moves between devices by JAX's collectives and lax.ppermute only.
A program may use at most 192 MiB of HBM per device.

v0:
```python
import jax
import jax.numpy as jnp
from jax import lax
from jax.sharding import PartitionSpec as P


def gelu_slope(values):
    inside = 0.7978845608028654 * (values + 0.044715 * values * values * values)
    curved = jnp.tanh(inside)
    return 0.5 * (1.0 + curved) + 0.5 * values * (1.0 - curved * curved) * 0.7978845608028654 * (
        1.0 + 3.0 * 0.044715 * values * values
    )


def body(grad_out, gate, expert_ids, w_in, w_out, pre_act):
    groups = lax.axis_size("expert")
    slots = pre_act.shape[2]
    capacity = slots // groups
    width = grad_out.shape[1]
    chosen = expert_ids[:, 0]
    hit_table = (chosen[:, None] == jnp.arange(groups, dtype=jnp.int32)[None, :]).astype(jnp.int32)
    position = jnp.sum(jnp.cumsum(hit_table, axis=0) * hit_table, axis=1) - 1
    target = chosen * capacity + position
    scaled = (grad_out.astype(jnp.float32) * gate).astype(jnp.bfloat16)
    outgoing = (
        jnp.zeros((slots, width), jnp.bfloat16)
        .at[target]
        .set(scaled)
        .reshape(groups, capacity, width)
    )
    arrived = lax.all_to_all(outgoing, "expert", split_axis=0, concat_axis=0, tiled=True)
    rows_in = arrived.reshape(slots, width)
    stashed = pre_act[0, 0]
    hidden_grad = jnp.einsum(
        "sd,fd->sf",
        rows_in,
        lax.all_gather(w_out, "dp", axis=1, tiled=True)[0],
        preferred_element_type=jnp.float32,
    )
    act_grad = (hidden_grad * gelu_slope(stashed.astype(jnp.float32))).astype(jnp.bfloat16)
    slot_sum = jnp.einsum(
        "sf,fd->sd",
        act_grad,
        lax.all_gather(w_in, "dp", axis=1, tiled=True)[0],
        preferred_element_type=jnp.float32,
    )
    slot_grad = slot_sum.astype(jnp.bfloat16).reshape(groups, capacity, width)
    returned = lax.all_to_all(slot_grad, "expert", split_axis=0, concat_axis=0, tiled=True)
    return returned.reshape(slots, width)[target]


def solution(mesh):
    return jax.shard_map(
        body,
        mesh=mesh,
        in_specs=(
            P(("dp", "expert"), None),
            P(("dp", "expert"), None),
            P(("dp", "expert"), None),
            P("expert", "dp", None),
            P("expert", "dp", None),
            P("dp", "expert", None, None),
        ),
        out_specs=P(("dp", "expert"), None),
        check_vma=False,
    )
```

profile of v0, /device:TPU:8, one launch (start us, length us, event | category | flops | bytes accessed | tf_op | source)
XLA Modules:
  0.0 312.6 jit_solution(17426288469553297094)
XLA Ops:
  6.5 0.0 all-gather.3.cloned.1.call-start
  6.5 0.7 all-gather.3.cloned.1.call-update
  7.3 0.0 all-gather.5.cloned.1.call-start
  7.3 0.7 all-gather.5.cloned.1.call-update
  8.0 0.7 fusion.23
  8.8 0.2 reduce_window_sum.11
  8.9 0.8 select_reduce_fusion
  9.8 0.7 fusion.24
  10.4 2.1 scatter_custom_fusion
  12.5 0.2 reshape.23
  12.8 22.9 %all_to_all.10 = bf16[16,10,2048]{2,1,0:T(8,128)(2,1)S(1)} all-to-all(bf16[16,10,2048]{2,1,0:T(8,128)(2,1)S(1)} %reshape.23), channel_id=1, replica_groups=mesh['dp'=32,'expert'=16] {'expert'}, dimensions={0} | all-to-all | bytes 1310720 | tf_op jit(solution)/shard_map/all_to_all | solution.py:31
  35.7 0.2 reshape.24
  35.9 105.8 %all-gather.3.cloned.1.call-done = bf16[1,5120,2048]{2,1,0:T(8,128)(2,1)} async-done(((bf16[1,160,2048]{2,1,0:T(8,128)(2,1)}), bf16[1,5120,2048]{2,1,0:T(8,128)(2,1)}) %all-gather.3.cloned.1.call-update) | async-done | bytes 20971536 | tf_op jit(solution)/shard_map/all_gather | solution.py:37
  141.7 12.6 %fusion.7 = bf16[160,5120]{1,0:T(8,128)(2,1)S(1)} fusion(bf16[160,2048]{1,0:T(8,128)(2,1)S(1)} %reshape.24, bf16[1,5120,2048]{2,1,0:T(8,128)(2,1)} %all-gather.3.cloned.1.call-done, bf16[1,1,160,5120]{3,2,1,0:T(8,128)(2,1)} %param.11), kind=kOutput, calls=%fused_computation.14 | convolution fusion | flops 3371827200 | bytes 24903680 | tf_op jit(solution)/shard_map/sd,fd->sf/dot_general | solution.py:34
  154.3 115.2 %all-gather.5.cloned.1.call-done = bf16[1,5120,2048]{2,1,0:T(8,128)(2,1)} async-done(((bf16[1,160,2048]{2,1,0:T(8,128)(2,1)}), bf16[1,5120,2048]{2,1,0:T(8,128)(2,1)}) %all-gather.5.cloned.1.call-update) | async-done | bytes 20971536 | tf_op jit(solution)/shard_map/all_gather | solution.py:44
  269.5 9.0 %fusion.17 = bf16[160,2048]{1,0:T(8,128)(2,1)S(1)} fusion(bf16[160,5120]{1,0:T(8,128)(2,1)S(1)} %fusion.7, bf16[1,5120,2048]{2,1,0:T(8,128)(2,1)} %all-gather.5.cloned.1.call-done), kind=kOutput, calls=%fused_computation.22 | convolution fusion | flops 3355770880 | bytes 23265280 | tf_op jit(solution)/shard_map/sf,fd->sd/dot_general | solution.py:41
  278.5 1.2 reshape.25
  279.7 7.3 %all-to-all-start.1 = ((bf16[16,10,2048]{2,1,0:T(8,128)(2,1)}), bf16[16,10,2048]{2,1,0:T(8,128)(2,1)S(1)}, u32[]{:S(2)}, u32[]{:S(2)}) async-start(bf16[16,10,2048]{2,1,0:T(8,128)(2,1)} %reshape.25), calls=%async_computation.1 | async-start | bytes 2097152 | tf_op jit(solution)/shard_map/all_to_all | solution.py:48
  287.0 16.8 %all-to-all-done.1 = bf16[16,10,2048]{2,1,0:T(8,128)(2,1)S(1)} async-done(((bf16[16,10,2048]{2,1,0:T(8,128)(2,1)}), bf16[16,10,2048]{2,1,0:T(8,128)(2,1)S(1)}, u32[]{:S(2)}, u32[]{:S(2)}) %all-to-all-start.1) | async-done | bytes 655392 | tf_op jit(solution)/shard_map/all_to_all | solution.py:48
  303.8 0.2 reshape.26
  304.0 1.7 gather_fusion
  (1 shorter events, 0.0 us)
Async XLA Ops:
  6.5 135.2 %all-gather.3.cloned.1.call-start = ((), (), s32[]{:S(2)}) async-start(), calls=%async_computation.2 | async-start | bytes 21626880 | tf_op jit(solution)/shard_map/all_gather | solution.py:37
  7.3 262.3 %all-gather.5.cloned.1.call-start = ((), (), s32[]{:S(2)}) async-start(), calls=%async_computation.3 | async-start | bytes 21626880 | tf_op jit(solution)/shard_map/all_gather | solution.py:44
  279.7 24.1 %all-to-all-start.1 = ((bf16[16,10,2048]{2,1,0:T(8,128)(2,1)}), bf16[16,10,2048]{2,1,0:T(8,128)(2,1)S(1)}, u32[]{:S(2)}, u32[]{:S(2)}) async-start(bf16[16,10,2048]{2,1,0:T(8,128)(2,1)} %reshape.25), calls=%async_computation.1 | async-start | bytes 2097152 | tf_op jit(solution)/shard_map/all_to_all | solution.py:48
Sparse Core Ops, SparseCore 0:
  9.5 132.2 all-gather.2
  143.8 125.6 all-gather.4
where the time goes:
time: 313 us
  waiting for transfers between devices  239 us (76%)
  blocking collectives  22.9 us (7%)
  matrix products  21.6 us (7%)
  between operations  13.5 us (4%)
  starting transfers between devices  7.29 us (2%)
  other arithmetic  4.53 us (1%)
  local copies, waits for them, and re-layouts  3.59 us (1%)
    all_gather x1, waiting for transfers between devices, body(): lax.all_gather(w_in, 'dp', axis=1, tiled=True)[0]  115 us
    all_gather x1, waiting for transfers between devices, body(): lax.all_gather(w_out, 'dp', axis=1, tiled=True)[0]  106 us
    all_to_all x1, blocking collectives, body(): lax.all_to_all(outgoing, 'expert', split_axis=0, concat_axis=0, tiled=True)  22.9 us
    all_to_all x1, waiting for transfers between devices, body(): lax.all_to_all(slot_grad, 'expert', split_axis=0, concat_axis=0, tiled=True)  16.8 us
    dot_general x1, matrix products, body(): jnp.einsum('sd,fd->sf', rows_in, lax.all_gather(w_out, 'dp', axis=1, tile...  12.6 us
    dot_general x1, matrix products, body(): jnp.einsum('sf,fd->sd', act_grad, lax.all_gather(w_in, 'dp', axis=1, tile...  8.95 us
    all_to_all x1, starting transfers between devices, body(): lax.all_to_all(slot_grad, 'expert', split_axis=0, concat_axis=0, tiled=True)  7.25 us
  transfers between devices with their start and end apart: 3, of which 3 were waited for; matrix products, arithmetic and copies ran while one was open for 6% of the time, Pallas kernels for 0%

commit v1 on v0

--- a/solution.py
+++ b/solution.py
@@ -34,7 +34,9 @@
     hidden_grad = jnp.einsum(
         "sd,fd->sf",
         rows_in,
-        lax.all_gather(w_out, "dp", axis=1, tiled=True)[0],
+        jnp.concatenate(
+            lax.all_to_all(jnp.stack([w_out] * lax.axis_size("dp")), "dp", 0, 0), axis=1
+        )[0],
         preferred_element_type=jnp.float32,
     )
     act_grad = (hidden_grad * gelu_slope(stashed.astype(jnp.float32))).astype(jnp.bfloat16)

time: 313 us -> 1130 us (3.61)
  the two profiles are of different devices: /device:TPU:8 before, /device:TPU:32 now
where the time goes in v1:
time: 1130 us
  waiting for transfers between devices  1030 us (91%)
  matrix products  24.4 us (2%)
  blocking collectives  23.7 us (2%)
  starting transfers between devices  19.4 us (2%)
  between operations  13.5 us (1%)
    all_to_all x1, waiting for transfers between devices, body(): lax.all_to_all(jnp.stack([w_out] * lax.axis_size('dp')), 'dp', 0, 0)  1010 us
    all_to_all x1, blocking collectives, body(): lax.all_to_all(outgoing, 'expert', split_axis=0, concat_axis=0, tiled=True)  23.7 us
  transfers between devices with their start and end apart: 3, of which 2 were waited for; matrix products, arithmetic and copies ran while one was open for 1% of the time, Pallas kernels for 0%

profile of v1, /device:TPU:32, one launch (start us, length us, event | category | flops | bytes accessed | tf_op | source)
XLA Modules:
  0.0 1127.0 jit_solution(9865189509837379109)
XLA Ops:
  6.5 0.0 copy-start
  6.5 0.8 fusion.16
  7.3 0.2 reduce_window_sum.11
  7.5 0.8 select_reduce_fusion
  8.3 0.7 fusion.17
  9.0 2.1 scatter_custom_fusion
  11.1 0.2 reshape.26
  11.4 23.7 %all_to_all.15 = bf16[16,10,2048]{2,1,0:T(8,128)(2,1)S(1)} all-to-all(bf16[16,10,2048]{2,1,0:T(8,128)(2,1)S(1)} %reshape.26), channel_id=1, replica_groups=mesh['dp'=32,'expert'=16] {'expert'}, dimensions={0} | all-to-all | bytes 1310720 | tf_op jit(solution)/shard_map/all_to_all | solution.py:31
  35.0 0.0 copy-done
  35.0 7.4 stack.2
  42.5 0.0 copy-start.1
  42.5 15.5 %all-to-all-start.1 = ((bf16[32,1,160,2048]{3,2,1,0:T(8,128)(2,1)}), bf16[32,1,160,2048]{3,2,1,0:T(8,128)(2,1)}, u32[]{:S(2)}, u32[]{:S(2)}) async-start(bf16[32,1,160,2048]{3,2,1,0:T(8,128)(2,1)} %stack.2), calls=%async_computation.1 | async-start | bytes 41943040 | tf_op jit(solution)/shard_map/all_to_all | solution.py:38
  58.0 0.0 all-gather.2.cloned.1.call-start
  58.0 0.7 all-gather.2.cloned.1.call-update
  58.7 0.2 reshape.27
  59.0 1012.5 %all-to-all-done.1 = bf16[32,1,160,2048]{3,2,1,0:T(8,128)(2,1)} async-done(((bf16[32,1,160,2048]{3,2,1,0:T(8,128)(2,1)}), bf16[32,1,160,2048]{3,2,1,0:T(8,128)(2,1)}, u32[]{:S(2)}, u32[]{:S(2)}) %all-to-all-start.1) | async-done | bytes 20971552 | tf_op jit(solution)/shard_map/all_to_all | solution.py:38
  1071.5 0.0 copy-done.1
  1071.5 13.4 %fusion.2 = bf16[160,5120]{1,0:T(8,128)(2,1)} fusion(bf16[160,2048]{1,0:T(8,128)(2,1)S(1)} %reshape.27, bf16[5120,2048]{1,0:T(8,128)(2,1)} %bitcast.5, bf16[1,1,160,5120]{3,2,1,0:T(8,128)(2,1)S(1)} %copy-done.1), kind=kOutput, calls=%fused_computation.12 | convolution fusion | flops 3371827200 | bytes 24903680 | tf_op jit(solution)/shard_map/sd,fd->sf/dot_general | solution.py:34
  1084.9 0.0 all-gather.2.cloned.1.call-done
  1084.9 11.0 fusion.10
  1095.9 1.2 reshape.28
  1097.1 3.8 all-to-all-start.2
  1100.9 17.2 %all-to-all-done.2 = bf16[16,10,2048]{2,1,0:T(8,128)(2,1)S(1)} async-done(((bf16[16,10,2048]{2,1,0:T(8,128)(2,1)}), bf16[16,10,2048]{2,1,0:T(8,128)(2,1)S(1)}, u32[]{:S(2)}, u32[]{:S(2)}) %all-to-all-start.2) | async-done | bytes 655392 | tf_op jit(solution)/shard_map/all_to_all | solution.py:50
  1118.2 0.2 reshape.29
  1118.4 1.7 gather_fusion
  (1 shorter events, 0.0 us)
Async XLA Ops:
  6.5 28.5 %copy-start = (bf16[1,160,2048]{2,1,0:T(8,128)(2,1)S(1)}, bf16[1,160,2048]{2,1,0:T(8,128)(2,1)}, u32[]{:S(2)}) copy-start(bf16[1,160,2048]{2,1,0:T(8,128)(2,1)} %param.10) | copy-start | bytes 1966084
  42.5 1029.0 %copy-start.1 = (bf16[1,1,160,5120]{3,2,1,0:T(8,128)(2,1)S(1)}, bf16[1,1,160,5120]{3,2,1,0:T(8,128)(2,1)}, u32[]{:S(2)}) copy-start(bf16[1,1,160,5120]{3,2,1,0:T(8,128)(2,1)} %param.11) | copy-start | bytes 4915204
  42.5 1029.0 %all-to-all-start.1 = ((bf16[32,1,160,2048]{3,2,1,0:T(8,128)(2,1)}), bf16[32,1,160,2048]{3,2,1,0:T(8,128)(2,1)}, u32[]{:S(2)}, u32[]{:S(2)}) async-start(bf16[32,1,160,2048]{3,2,1,0:T(8,128)(2,1)} %stack.2), calls=%async_computation.1 | async-start | bytes 41943040 | tf_op jit(solution)/shard_map/all_to_all | solution.py:38
  58.0 1026.9 %all-gather.2.cloned.1.call-start = ((), (), s32[]{:S(2)}) async-start(), calls=%async_computation.3 | async-start | bytes 21626880 | tf_op jit(solution)/shard_map/all_gather | solution.py:46
  1097.1 21.1 %all-to-all-start.2 = ((bf16[16,10,2048]{2,1,0:T(8,128)(2,1)}), bf16[16,10,2048]{2,1,0:T(8,128)(2,1)S(1)}, u32[]{:S(2)}, u32[]{:S(2)}) async-start(bf16[16,10,2048]{2,1,0:T(8,128)(2,1)} %reshape.28), calls=%async_computation.2 | async-start | bytes 2097152 | tf_op jit(solution)/shard_map/all_to_all | solution.py:50
Sparse Core Ops, SparseCore 0:
  60.9 581.1 all-gather.1
